TPU v7x, 32 devices: a whole 2x2x4 slice. The times are simulated.
32 devices in a mesh: member: 1, lat: 32 (over z, y, x, core).
Axes of the slice: x: 2, y: 2, z: 4, core: 2. Of those that a mesh axis runs over, the one named last changes fastest.
Arguments:
- spectral: bfloat16 [512, 512, 256], P(('member', 'lat')), may hold values from -6 to 6
- lat_basis: bfloat16 [512, 512, 192], P('lat'), may hold values from -0.0078125 to 0.0078125
- block_order: int32 [128], replicated, may hold values from 0 to 127, each once
- in_weight: bfloat16 [128, 1024], replicated, may hold values from -0.5 to 0.5
- in_bias: float32 [1024], replicated, may hold values from -3 to 3
- out_weight: bfloat16 [1024, 128], replicated, may hold values from -0.1875 to 0.1875
- col_gain: float32 [128], replicated, may hold values from 0.5 to 2
- damping: float32 [128], replicated, may hold values from 0.2 to 2
Outputs:
- tendency: float32 [512, 512, 256], P(('member', 'lat'))
Inputs may be any that keep to these rules, and one draw needn't show every extreme that they name: `block_order`: each wavenumber block appears exactly once.
All inputs are finite; a program needn't handle non-finite values.
Results may differ from a plain program's by a relative error of at most 0.004.
The roundings to bfloat16 on the way count: a program that leaves them out, or rounds other values in their place, can miss the bound.
Values may be sent and summed in bfloat16 or wider, within the bound.
No kernel may reach another device: no remote copies, remote signals or barrier semaphores. Data moves between devices by JAX's collectives and lax.ppermute only.
A program may use at most 128 MiB of HBM per device.

v0:
```python
import math
import jax
import jax.numpy as jnp
from jax import lax
from jax.sharding import PartitionSpec as P

NN = 512
NLON = 1536
MB = 4


def wavenumbers(block_order, slot_count):
    slot_ids = jnp.arange(slot_count, dtype=jnp.int32)
    blocks = block_order.shape[0]
    matches = (slot_ids // MB)[:, None] == jnp.arange(blocks, dtype=jnp.int32)[None, :]
    chosen = jnp.sum(jnp.where(matches, block_order[None, :], 0), axis=1)
    return chosen * MB + slot_ids % MB


def lon_table(wave_all):
    longitude = jnp.arange(NLON, dtype=jnp.int32)
    phase_index = wave_all[:, None] * longitude[None, :] % NLON
    angles = phase_index.astype(jnp.float32) * (2.0 * math.pi / NLON)
    return jnp.concatenate([jnp.cos(angles), jnp.sin(angles)], axis=0).astype(jnp.bfloat16)


def lat_weights(first_lat, lat_count, lat_total):
    latitude = (first_lat + jnp.arange(lat_count, dtype=jnp.int32)).astype(jnp.float32)
    return jnp.cos(math.pi * ((latitude + 0.5) / lat_total - 0.5))


def on_device(spectral, lat_basis, block_order, in_weight, in_bias, out_weight, col_gain, damping):
    devices = lax.axis_size("lat")
    my_index = lax.axis_index("lat")
    row_count = spectral.shape[0]
    degrees = spectral.shape[1]
    chan_width = spectral.shape[2]
    chan_count = chan_width // 2
    half_lat = lat_basis.shape[2]
    lat_total = 2 * half_lat
    lat_local = lat_total // devices
    wave_total = row_count * devices
    wave_all = wavenumbers(block_order, wave_total)
    wave_own = lax.dynamic_slice_in_dim(wave_all, my_index * row_count, row_count)
    degree = jnp.arange(degrees, dtype=jnp.int32)
    inside = degree[None, :] >= wave_own[:, None]
    parity = jnp.where((degree[None, :] + wave_own[:, None]) % 2 == 0, 1.0, -1.0).astype(
        jnp.float32
    )
    masked = jnp.where(inside[:, :, None], spectral, jnp.zeros_like(spectral))
    flipped = jnp.where(parity[:, :, None] > 0, masked, -masked)
    north_half = jnp.einsum("rnj,rnc->jrc", lat_basis, masked, preferred_element_type=jnp.float32)
    south_half = jnp.einsum("rnj,rnc->jrc", lat_basis, flipped, preferred_element_type=jnp.float32)
    fourier = jnp.concatenate([north_half, south_half[::-1]], axis=0).astype(jnp.bfloat16)
    outbound = fourier.reshape(devices, lat_local, row_count, chan_width)
    wave_table = lon_table(wave_all)
    rows_in = lax.all_to_all(outbound, "lat", split_axis=0, concat_axis=2, tiled=True)[0]
    signed = jnp.concatenate([rows_in[:, :, :chan_count], -rows_in[:, :, chan_count:]], axis=1)
    grid_field = jnp.einsum(
        "jrk,rl->jkl", signed, wave_table, preferred_element_type=jnp.float32
    ).astype(jnp.bfloat16)
    weight_own = lat_weights(my_index * lat_local, lat_local, lat_total)
    grid_wide = grid_field.astype(jnp.float32)
    partial_value = jnp.sum(weight_own[:, None, None] * grid_wide * grid_wide, axis=(0, 2))
    global_sum = lax.psum(partial_value, "lat")
    weight_all = lat_weights(0, lat_total, lat_total)
    variance = global_sum / (NLON * jnp.sum(weight_all))
    col_scale = col_gain * lax.rsqrt(variance + 1e-05)
    inv_root = 1.0 / math.sqrt(NLON)
    contract_first = (((0,), (0,)), ((), ()))

    def column(row_grid):
        normed = (row_grid.astype(jnp.float32) * col_scale[:, None]).astype(jnp.bfloat16)
        hidden = jax.nn.gelu(
            lax.dot_general(in_weight, normed, contract_first, preferred_element_type=jnp.float32)
            + in_bias[:, None]
        ).astype(jnp.bfloat16)
        column_out = lax.dot_general(
            out_weight, hidden, contract_first, preferred_element_type=jnp.float32
        ).astype(jnp.bfloat16)
        back_proj = lax.dot_general(
            wave_table, column_out, (((1,), (1,)), ((), ())), preferred_element_type=jnp.float32
        )
        return (
            jnp.concatenate([back_proj[:wave_total], -back_proj[wave_total:]], axis=1) * inv_root
        ).astype(jnp.bfloat16)

    coeffs = lax.map(column, grid_field)
    returning = coeffs.reshape(lat_local, devices, row_count, chan_width)
    factor = 2.0 * math.sqrt(degrees * wave_total / lat_total)
    weighted = (
        weight_all[:, None, None]
        * lax.all_to_all(returning, "lat", split_axis=1, concat_axis=0, tiled=True)[:, 0].astype(
            jnp.float32
        )
    ).astype(jnp.bfloat16)
    north_part = weighted[:half_lat]
    south_part = weighted[half_lat:][::-1]
    east_sum = jnp.einsum("rnj,jrc->rnc", lat_basis, north_part, preferred_element_type=jnp.float32)
    west_sum = jnp.einsum("rnj,jrc->rnc", lat_basis, south_part, preferred_element_type=jnp.float32)
    legendre = factor * (east_sum + parity[:, :, None] * west_sum)
    damp_all = jnp.concatenate([damping, damping])
    wave_factor = (degree * (degree + 1)).astype(jnp.float32) / (NN * NN)
    damped = legendre - damp_all[None, None, :] * wave_factor[None, :, None] * spectral.astype(
        jnp.float32
    )
    return jnp.where(inside[:, :, None], damped, jnp.zeros_like(damped))


def solution(mesh):
    in_specs = (
        P(("member", "lat"), None, None),
        P("lat", None, None),
        P(),
        P(),
        P(),
        P(),
        P(),
        P(),
    )
    out_specs = P(("member", "lat"), None, None)
    return jax.shard_map(
        on_device, mesh=mesh, in_specs=in_specs, out_specs=out_specs, check_vma=False
    )
```

profile of v0, /device:TPU:0, one launch (start us, length us, event | category | flops | bytes accessed | tf_op | source)
XLA Modules:
  0.0 446.9 jit_solution(13777267566337233392)
XLA Ops:
  1.2 6.4 %copy.40 = bf16[16,512,256]{1,2,0:T(8,128)(2,1)} copy(bf16[16,512,256]{2,1,0:T(8,128)(2,1)} %param.10) | data formatting | bytes 8388608 | tf_op args[0]
  7.7 5.0 %fusion.46 = bf16[192,16,256]{2,0,1:T(8,128)(2,1)} fusion(bf16[16,512,192]{1,2,0:T(8,128)(2,1)S(1)} %copy-done, bf16[16,512,256]{1,2,0:T(8,128)(2,1)} %copy.40, pred[16,512]{1,0:T(8,128)(4,1)S(1)} %get-tuple-element.70), kind=kOutput, calls=%fused_computation.61 | convolution fusion | flops 808189952 | bytes 8921088 | tf_op jit(solution)/shard_map/rnj,rnc->jrc/dot_general | solution.py:52
  12.7 2.7 fusion.42
  15.4 29.9 %rev.6 = bf16[192,16,256]{2,0,1:T(8,128)(2,1)} reverse(bf16[192,16,256]{2,0,1:T(8,128)(2,1)} %fusion.42), dimensions={0} | reverse | bytes 3145728 | tf_op jit(solution)/shard_map/rev | solution.py:54
  47.5 3.5 copy.43
  50.9 7.6 %all-to-all-start = ((bf16[32,12,16,256]{3,2,1,0:T(8,128)(2,1)}), bf16[32,12,16,256]{3,2,1,0:T(8,128)(2,1)}, u32[]{:S(2)}, u32[]{:S(2)}) async-start(bf16[32,12,16,256]{3,2,1,0:T(8,128)(2,1)} %bitcast.68), calls=%async_computation | async-start | bytes 6291456 | tf_op jit(solution)/shard_map/all_to_all | solution.py:57
  59.9 13.5 %cosine_convert_fusion = (bf16[512,1536]{1,0:T(8,128)(2,1)S(1)}, bf16[512,1536]{1,0:T(8,128)(2,1)S(1)}) fusion(s32[512]{0:T(512)S(1)} %fusion.59), kind=kLoop, calls=%fused_computation.50 | loop fusion | flops 8650752 | bytes 3147776 | tf_op jit(solution)/shard_map/convert.4
  77.0 52.9 %all-to-all-done = bf16[32,12,16,256]{3,2,1,0:T(8,128)(2,1)} async-done(((bf16[32,12,16,256]{3,2,1,0:T(8,128)(2,1)}), bf16[32,12,16,256]{3,2,1,0:T(8,128)(2,1)}, u32[]{:S(2)}, u32[]{:S(2)}) %all-to-all-start) | async-done | bytes 3145760 | tf_op jit(solution)/shard_map/all_to_all | solution.py:57
  132.1 2.5 fusion.67
  134.6 2.6 copy.57
  137.2 2.9 neg.10
  140.1 2.6 copy.56
  142.7 10.3 %fusion.25 = (f32[128]{0:T(128)S(1)}, bf16[12,128,1536]{2,1,0:T(8,128)(2,1)}) fusion(f32[12]{0:T(128)S(1)} %multiply_cosine_fusion.1, bf16[512,1536]{1,0:T(8,128)(2,1)} %copy-done.3, bf16[512,1536]{1,0:T(8,128)(2,1)} %copy-done.2, bf16[12,512,128]{1,2,0:T(8,128)(2,1)} %neg.10, bf16[12,512,128]{1,2,0:T(8,128)(2,1)} %copy.56), kind=kOutput, calls=%fused_computation.28 | convolution fusion | flops 4856217600 | bytes 11010608 | tf_op jit(solution)/shard_map/jrk,rl->jkl/dot_general | solution.py:59
  153.0 38.1 %psum.7 = f32[128]{0:T(128)S(1)} all-reduce(f32[128]{0:T(128)S(1)} %get-tuple-element.72), channel_id=1, replica_groups=mesh['member'=1,'lat'=32] {'lat'}, use_global_device_ids=true, to_apply=%region_2.3 | all-reduce | flops 128 | bytes 1024 | tf_op jit(solution)/shard_map/psum | solution.py:65
  191.1 114.6 %while.10 = (s32[]{:T(128)}, bf16[12,512,256]{2,1,0:T(8,128)(2,1)}, bf16[12,128,1536]{2,1,0:T(8,128)(2,1)}, f32[128]{0:T(128)S(1)}, bf16[128,1024]{1,0:T(8,128)(...) while((s32[]{:T(128)}, bf16[12,512,256]{2,1,0:T(8,128)(2,1)}, ...), condition=%wide.region_5.6_spmd, body=%wide.region_4.5_spmd.sunk | while | flops 1224933376 | bytes 8263261 | solution.py:88
  191.1 3.9 convolution_convert_fusion.3
  195.0 3.0 convolution_bitcast_fusion.2
  200.7 3.9 convolution_convert_fusion.3
  204.6 3.0 convolution_bitcast_fusion.2
  210.2 3.9 convolution_convert_fusion.3
  214.1 3.0 convolution_bitcast_fusion.2
  219.8 3.9 convolution_convert_fusion.3
  223.7 3.0 convolution_bitcast_fusion.2
  229.4 3.9 convolution_convert_fusion.3
  233.3 3.0 convolution_bitcast_fusion.2
  238.9 3.9 convolution_convert_fusion.3
  242.8 3.0 convolution_bitcast_fusion.2
  248.5 3.9 convolution_convert_fusion.3
  252.4 3.0 convolution_bitcast_fusion.2
  258.0 3.9 convolution_convert_fusion.3
  261.9 3.0 convolution_bitcast_fusion.2
  267.5 3.9 convolution_convert_fusion.3
  271.4 3.0 convolution_bitcast_fusion.2
  277.1 3.9 convolution_convert_fusion.3
  281.0 3.0 convolution_bitcast_fusion.2
  286.6 3.9 convolution_convert_fusion.3
  290.5 3.0 convolution_bitcast_fusion.2
  296.2 3.9 convolution_convert_fusion.3
  300.1 3.0 convolution_bitcast_fusion.2
  305.8 4.0 copy.48
  309.7 5.1 %all-to-all-start.1 = ((bf16[12,32,16,256]{3,2,0,1:T(8,128)(2,1)}), bf16[12,32,16,256]{3,2,0,1:T(8,128)(2,1)}, u32[]{:S(2)}, u32[]{:S(2)}) async-start(bf16[12,32,16,256]{3,2,0,1:T(8,128)(2,1)} %copy.48), calls=%async_computation.1 | async-start | bytes 6291456 | tf_op jit(solution)/shard_map/all_to_all | solution.py:93
  316.0 70.4 %all-to-all-done.1 = bf16[12,32,16,256]{3,2,0,1:T(8,128)(2,1)} async-done(((bf16[12,32,16,256]{3,2,0,1:T(8,128)(2,1)}), bf16[12,32,16,256]{3,2,0,1:T(8,128)(2,1)}, u32[]{:S(2)}, u32[]{:S(2)}) %all-to-all-start.1) | async-done | bytes 3145760 | tf_op jit(solution)/shard_map/all_to_all | solution.py:93
  386.3 2.7 bitcast_convert_fusion
  389.1 4.0 fusion.27
  393.0 4.8 %fusion.44 = f32[16,256,512]{2,1,0:T(8,128)} fusion(bf16[16,512,192]{1,2,0:T(8,128)(2,1)S(1)} %copy-done, bf16[384,16,256]{2,0,1:T(8,128)(2,1)S(1)} %fusion.27), kind=kOutput, calls=%fused_computation.59 | convolution fusion | flops 805306368 | bytes 13107200 | tf_op jit(solution)/shard_map/rnj,jrc->rnc/dot_general | solution.py:99
  399.1 29.9 %rev.7 = bf16[192,16,256]{2,0,1:T(8,128)(2,1)} reverse(bf16[192,16,256]{2,0,1:T(8,128)(2,1)} %slice.27), dimensions={0} | reverse | bytes 3145728 | tf_op jit(solution)/shard_map/rev | solution.py:98
  429.0 8.7 %fusion.26 = f32[16,512,256]{1,2,0:T(8,128)} fusion(bf16[16,512,256]{1,2,0:T(8,128)(2,1)} %copy.40, f32[16,256,512]{2,1,0:T(8,128)} %fusion.44, f32[512,256]{0,1:T(8,128)} %broadcast_multiply_fusion, f32[16,512]{1,0:T(8,128)S(1)} %fusion.51, pred[16,512]{1,0:T(8,128)(4,1)S(1)} %get-tuple-element.70, bf16[192,16,256]{2,0,1:T(8,128)(2,1)} %rev.7, ...), kind=kOutput, calls=%fused_computation.30 | convolution fusion | flops 819986432 | bytes 26255360 | tf_op jit(solution)/shard_map/rnj,jrc->rnc/dot_general | solution.py:100
  437.7 9.2 %copy.51 = f32[16,512,256]{2,1,0:T(8,128)} copy(f32[16,512,256]{1,2,0:T(8,128)} %fusion.26) | data formatting | bytes 16777216 | tf_op jit(solution)/shard_map/jit(_where)/select_n | solution.py:107
  (78 shorter events, 43.3 us)
Async XLA Ops:
  0.0 7.7 %copy-start = (bf16[16,512,192]{1,2,0:T(8,128)(2,1)S(1)}, bf16[16,512,192]{1,2,0:T(8,128)(2,1)}, u32[]{:S(2)}) copy-start(bf16[16,512,192]{1,2,0:T(8,128)(2,1)} %param.11) | copy-start | bytes 9437188
  7.7 5.0 %copy-start.1 = (bf16[16,512,256]{1,2,0:T(8,128)(2,1)S(1)}, bf16[16,512,256]{1,2,0:T(8,128)(2,1)}, u32[]{:S(2)}) copy-start(bf16[16,512,256]{1,2,0:T(8,128)(2,1)} %copy.40) | copy-start | bytes 12582916
  50.9 78.9 %all-to-all-start = ((bf16[32,12,16,256]{3,2,1,0:T(8,128)(2,1)}), bf16[32,12,16,256]{3,2,1,0:T(8,128)(2,1)}, u32[]{:S(2)}, u32[]{:S(2)}) async-start(bf16[32,12,16,256]{3,2,1,0:T(8,128)(2,1)} %bitcast.68), calls=%async_computation | async-start | bytes 6291456 | tf_op jit(solution)/shard_map/all_to_all | solution.py:57
  73.4 1.2 copy-start.2
  73.4 1.7 copy-start.3
  142.7 48.4 %copy-start.4 = (f32[128]{0:T(128)S(1)}, f32[128]{0:T(128)}, u32[]{:S(2)}) copy-start(f32[128]{0:T(128)} %param.16) | copy-start | bytes 1540
  309.7 5.2 %copy-start.5 = (f32[128]{0:T(128)S(1)}, f32[128]{0:T(128)}, u32[]{:S(2)}) copy-start(f32[128]{0:T(128)} %param.17) | copy-start | bytes 1540
  309.7 76.6 %all-to-all-start.1 = ((bf16[12,32,16,256]{3,2,0,1:T(8,128)(2,1)}), bf16[12,32,16,256]{3,2,0,1:T(8,128)(2,1)}, u32[]{:S(2)}, u32[]{:S(2)}) async-start(bf16[12,32,16,256]{3,2,0,1:T(8,128)(2,1)} %copy.48), calls=%async_computation.1 | async-start | bytes 6291456 | tf_op jit(solution)/shard_map/all_to_all | solution.py:93
where the time goes:
time: 455 us; the launch traced here: 447 us
  local copies, waits for them, and re-layouts  126 us (28%)
  waiting for transfers between devices  123 us (27%)
  matrix products  115 us (25%)
  blocking collectives  38.1 us (8%)
  other arithmetic  31.1 us (7%)
  starting transfers between devices  12.7 us (3%)
    all_to_all x1, waiting for transfers between devices, on_device(): lax.all_to_all(returning, 'lat', split_axis=1, concat_axis=0, tiled=True)  70.4 us
    all_to_all x1, waiting for transfers between devices, on_device(): lax.all_to_all(outbound, 'lat', split_axis=0, concat_axis=2, tiled=True)[0]  52.9 us
    dot_general x12, matrix products, column(): lax.dot_general(out_weight, hidden, contract_first, preferred_element_typ...  46.7 us
    psum x1, blocking collectives, on_device(): global_sum = lax.psum(partial_value, 'lat')  38.1 us
    dot_general x12, matrix products, column(): lax.dot_general(wave_table, column_out, (((1,), (1,)), ((), ())), preferr...  36.5 us
    dynamic_update_slice x24, local copies, waits for them, and re-layouts, on_device(): coeffs = lax.map(column, grid_field)  30.1 us
    rev x1, local copies, waits for them, and re-layouts, on_device(): south_part = weighted[half_lat:][::-1]  29.9 us
    rev x1, local copies, waits for them, and re-layouts, on_device(): south_half[::-1]  29.9 us
  transfers between devices with their start and end apart: 2, of which 2 were waited for; matrix products, arithmetic and copies ran while one was open for 4% of the time, Pallas kernels for 0%

commit v1 on v0

--- a/solution.py
+++ b/solution.py
@@ -54,7 +54,10 @@
     fourier = jnp.concatenate([north_half, south_half[::-1]], axis=0).astype(jnp.bfloat16)
     outbound = fourier.reshape(devices, lat_local, row_count, chan_width)
     wave_table = lon_table(wave_all)
-    rows_in = lax.all_to_all(outbound, "lat", split_axis=0, concat_axis=2, tiled=True)[0]
+    rows_in = jnp.concatenate(
+        lax.all_to_all(jnp.stack(jnp.split(outbound, lax.axis_size("lat"), axis=0)), "lat", 0, 0),
+        axis=2,
+    )[0]
     signed = jnp.concatenate([rows_in[:, :, :chan_count], -rows_in[:, :, chan_count:]], axis=1)
     grid_field = jnp.einsum(
         "jrk,rl->jkl", signed, wave_table, preferred_element_type=jnp.float32

time: 455 us -> 490 us (1.077)
  local copies, waits for them, and re-layouts: 126 us -> 164 us
    unnamed x15 -> x46, local copies, waits for them, and re-layouts: 13.3 us -> 48.1 us
    another operation x0 -> x2, local copies, waits for them, and re-layouts: none -> 6.85 us  [on_device(): jnp.stack(jnp.split(outbound, lax.axis_size('lat'), axis=0))]
where the time goes in v1:
time: 490 us; the launch traced here: 482 us
  local copies, waits for them, and re-layouts  164 us (33%)
  waiting for transfers between devices  123 us (25%)
  matrix products  114 us (23%)
  blocking collectives  38.1 us (8%)
  other arithmetic  28.9 us (6%)
  starting transfers between devices  12.7 us (3%)
    all_to_all x1, waiting for transfers between devices, on_device(): lax.all_to_all(returning, 'lat', split_axis=1, concat_axis=0, tiled=True)  70.4 us
    all_to_all x1, waiting for transfers between devices, on_device(): lax.all_to_all(jnp.stack(jnp.split(outbound, lax.axis_size('lat'), axis=0...  52.8 us
    unnamed x46, local copies, waits for them, and re-layouts  48.1 us
    dot_general x12, matrix products, column(): lax.dot_general(out_weight, hidden, contract_first, preferred_element_typ...  46.7 us
    psum x1, blocking collectives, on_device(): global_sum = lax.psum(partial_value, 'lat')  38.1 us
    dot_general x12, matrix products, column(): lax.dot_general(wave_table, column_out, (((1,), (1,)), ((), ())), preferr...  36.5 us
    dynamic_update_slice x24, local copies, waits for them, and re-layouts, on_device(): coeffs = lax.map(column, grid_field)  30.1 us
    rev x1, local copies, waits for them, and re-layouts, on_device(): south_part = weighted[half_lat:][::-1]  29.9 us
  transfers between devices with their start and end apart: 2, of which 2 were waited for; matrix products, arithmetic and copies ran while one was open for 4% of the time, Pallas kernels for 0%

profile of v1, /device:TPU:0, one launch (start us, length us, event | category | flops | bytes accessed | tf_op | source)
XLA Modules:
  0.0 481.7 jit_solution(4249654012387218475)
XLA Ops:
  1.2 6.4 %copy.49 = bf16[16,512,256]{1,2,0:T(8,128)(2,1)} copy(bf16[16,512,256]{2,1,0:T(8,128)(2,1)} %param.10) | data formatting | bytes 8388608 | tf_op args[0]
  7.7 3.7 fusion.46
  22.3 2.8 fusion.42
  25.1 29.8 %rev.6 = bf16[192,16,256]{2,0,1:T(8,128)(2,1)} reverse(bf16[192,16,256]{2,0,1:T(8,128)(2,1)} %fusion.42), dimensions={0} | reverse | bytes 3145728 | tf_op jit(solution)/shard_map/rev | solution.py:54
  80.5 5.3 %copy.52 = bf16[32,1,12,16,256]{4,3,2,1,0:T(8,128)(2,1)} copy(bf16[32,1,12,16,256]{4,2,3,1,0:T(8,128)(2,1)} %fusion.47) | data formatting | bytes 6291456 | tf_op jit(solution)/shard_map/stack | solution.py:58
  85.7 7.6 %all-to-all-start = ((bf16[32,1,12,16,256]{4,3,2,1,0:T(8,128)(2,1)}), bf16[32,1,12,16,256]{4,3,2,1,0:T(8,128)(2,1)}, u32[]{:S(2)}, u32[]{:S(2)}) async-start(bf16[32,1,12,16,256]{4,3,2,1,0:T(8,128)(2,1)} %copy.52), calls=%async_computation | async-start | bytes 6291456 | tf_op jit(solution)/shard_map/all_to_all | solution.py:58
  94.7 13.5 %cosine_convert_fusion = (bf16[512,1536]{1,0:T(8,128)(2,1)S(1)}, bf16[512,1536]{1,0:T(8,128)(2,1)S(1)}) fusion(s32[512]{0:T(512)S(1)} %fusion.91), kind=kLoop, calls=%fused_computation.49 | loop fusion | flops 8650752 | bytes 3147776 | tf_op jit(solution)/shard_map/convert.4
  111.8 52.8 %all-to-all-done = bf16[32,1,12,16,256]{4,3,2,1,0:T(8,128)(2,1)} async-done(((bf16[32,1,12,16,256]{4,3,2,1,0:T(8,128)(2,1)}), bf16[32,1,12,16,256]{4,3,2,1,0:T(8,128)(2,1)}, u32[]{:S(2)}, u32[]{:S(2)}) %all-to-all-start) | async-done | bytes 3145760 | tf_op jit(solution)/shard_map/all_to_all | solution.py:58
  166.9 2.5 fusion.99
  169.4 2.6 copy.66
  172.0 2.9 neg.10
  174.9 2.6 copy.65
  177.5 10.3 %fusion.25 = (f32[128]{0:T(128)S(1)}, bf16[12,128,1536]{2,1,0:T(8,128)(2,1)}) fusion(f32[12]{0:T(128)S(1)} %multiply_cosine_fusion.1, bf16[512,1536]{1,0:T(8,128)(2,1)} %copy-done.3, bf16[512,1536]{1,0:T(8,128)(2,1)} %copy-done.2, bf16[12,512,128]{1,2,0:T(8,128)(2,1)} %neg.10, bf16[12,512,128]{1,2,0:T(8,128)(2,1)} %copy.65), kind=kOutput, calls=%fused_computation.28 | convolution fusion | flops 4856217600 | bytes 11010608 | tf_op jit(solution)/shard_map/jrk,rl->jkl/dot_general | solution.py:62
  187.8 38.1 %psum.7 = f32[128]{0:T(128)S(1)} all-reduce(f32[128]{0:T(128)S(1)} %get-tuple-element.72), channel_id=1, replica_groups=mesh['member'=1,'lat'=32] {'lat'}, use_global_device_ids=true, to_apply=%region_2.3 | all-reduce | flops 128 | bytes 1024 | tf_op jit(solution)/shard_map/psum | solution.py:68
  225.9 114.6 %while.10 = (s32[]{:T(128)}, bf16[12,512,256]{2,1,0:T(8,128)(2,1)}, bf16[12,128,1536]{2,1,0:T(8,128)(2,1)}, f32[128]{0:T(128)S(1)}, bf16[128,1024]{1,0:T(8,128)(...) while((s32[]{:T(128)}, bf16[12,512,256]{2,1,0:T(8,128)(2,1)}, ...), condition=%wide.region_5.6_spmd, body=%wide.region_4.5_spmd.sunk | while | flops 1224933376 | bytes 8263261 | solution.py:91
  225.9 3.9 convolution_convert_fusion.3
  229.8 3.0 convolution_bitcast_fusion.2
  235.5 3.9 convolution_convert_fusion.3
  239.4 3.0 convolution_bitcast_fusion.2
  245.0 3.9 convolution_convert_fusion.3
  248.9 3.0 convolution_bitcast_fusion.2
  254.6 3.9 convolution_convert_fusion.3
  258.5 3.0 convolution_bitcast_fusion.2
  264.2 3.9 convolution_convert_fusion.3
  268.1 3.0 convolution_bitcast_fusion.2
  273.7 3.9 convolution_convert_fusion.3
  277.6 3.0 convolution_bitcast_fusion.2
  283.3 3.9 convolution_convert_fusion.3
  287.2 3.0 convolution_bitcast_fusion.2
  292.8 3.9 convolution_convert_fusion.3
  296.7 3.0 convolution_bitcast_fusion.2
  302.3 3.9 convolution_convert_fusion.3
  306.2 3.0 convolution_bitcast_fusion.2
  311.9 3.9 convolution_convert_fusion.3
  315.8 3.0 convolution_bitcast_fusion.2
  321.4 3.9 convolution_convert_fusion.3
  325.3 3.0 convolution_bitcast_fusion.2
  331.0 3.9 convolution_convert_fusion.3
  334.9 3.0 convolution_bitcast_fusion.2
  340.6 4.0 copy.57
  344.5 5.1 %all-to-all-start.1 = ((bf16[12,32,16,256]{3,2,0,1:T(8,128)(2,1)}), bf16[12,32,16,256]{3,2,0,1:T(8,128)(2,1)}, u32[]{:S(2)}, u32[]{:S(2)}) async-start(bf16[12,32,16,256]{3,2,0,1:T(8,128)(2,1)} %copy.57), calls=%async_computation.1 | async-start | bytes 6291456 | tf_op jit(solution)/shard_map/all_to_all | solution.py:96
  350.8 70.4 %all-to-all-done.1 = bf16[12,32,16,256]{3,2,0,1:T(8,128)(2,1)} async-done(((bf16[12,32,16,256]{3,2,0,1:T(8,128)(2,1)}), bf16[12,32,16,256]{3,2,0,1:T(8,128)(2,1)}, u32[]{:S(2)}, u32[]{:S(2)}) %all-to-all-start.1) | async-done | bytes 3145760 | tf_op jit(solution)/shard_map/all_to_all | solution.py:96
  421.1 2.7 bitcast_convert_fusion
  423.9 4.0 fusion.27
  427.8 4.8 fusion.44
  433.9 29.9 %rev.7 = bf16[192,16,256]{2,0,1:T(8,128)(2,1)} reverse(bf16[192,16,256]{2,0,1:T(8,128)(2,1)} %slice.91), dimensions={0} | reverse | bytes 3145728 | tf_op jit(solution)/shard_map/rev | solution.py:101
  463.8 8.7 %fusion.26 = f32[16,512,256]{1,2,0:T(8,128)} fusion(bf16[16,512,256]{1,2,0:T(8,128)(2,1)} %copy.49, f32[16,256,512]{2,1,0:T(8,128)} %fusion.44, f32[512,256]{0,1:T(8,128)} %broadcast_multiply_fusion, f32[16,512]{1,0:T(8,128)S(1)} %fusion.83, pred[16,512]{1,0:T(8,128)(4,1)S(1)} %get-tuple-element.71, bf16[192,16,256]{2,0,1:T(8,128)(2,1)} %rev.7, ...), kind=kOutput, calls=%fused_computation.30 | convolution fusion | flops 819986432 | bytes 26255360 | tf_op jit(solution)/shard_map/rnj,jrc->rnc/dot_general | solution.py:103
  472.4 9.2 %copy.60 = f32[16,512,256]{2,1,0:T(8,128)} copy(f32[16,512,256]{1,2,0:T(8,128)} %fusion.26) | data formatting | bytes 16777216 | tf_op jit(solution)/shard_map/jit(_where)/select_n | solution.py:110
  (109 shorter events, 77.5 us)
Async XLA Ops:
  0.0 7.7 %copy-start = (bf16[16,512,192]{1,2,0:T(8,128)(2,1)S(1)}, bf16[16,512,192]{1,2,0:T(8,128)(2,1)}, u32[]{:S(2)}) copy-start(bf16[16,512,192]{1,2,0:T(8,128)(2,1)} %param.11) | copy-start | bytes 9437188
  11.4 10.9 %copy-start.1 = (bf16[16,512,256]{1,2,0:T(8,128)(2,1)S(1)}, bf16[16,512,256]{1,2,0:T(8,128)(2,1)}, u32[]{:S(2)}) copy-start(bf16[16,512,256]{1,2,0:T(8,128)(2,1)} %copy.49) | copy-start | bytes 12582916
  85.7 78.9 %all-to-all-start = ((bf16[32,1,12,16,256]{4,3,2,1,0:T(8,128)(2,1)}), bf16[32,1,12,16,256]{4,3,2,1,0:T(8,128)(2,1)}, u32[]{:S(2)}, u32[]{:S(2)}) async-start(bf16[32,1,12,16,256]{4,3,2,1,0:T(8,128)(2,1)} %copy.52), calls=%async_computation | async-start | bytes 6291456 | tf_op jit(solution)/shard_map/all_to_all | solution.py:58
  108.2 1.2 copy-start.2
  108.2 1.7 copy-start.3
  177.5 48.4 %copy-start.4 = (f32[128]{0:T(128)S(1)}, f32[128]{0:T(128)}, u32[]{:S(2)}) copy-start(f32[128]{0:T(128)} %param.16) | copy-start | bytes 1540
  344.5 5.1 %copy-start.5 = (f32[128]{0:T(128)S(1)}, f32[128]{0:T(128)}, u32[]{:S(2)}) copy-start(f32[128]{0:T(128)} %param.17) | copy-start | bytes 1540
  344.5 76.6 %all-to-all-start.1 = ((bf16[12,32,16,256]{3,2,0,1:T(8,128)(2,1)}), bf16[12,32,16,256]{3,2,0,1:T(8,128)(2,1)}, u32[]{:S(2)}, u32[]{:S(2)}) async-start(bf16[12,32,16,256]{3,2,0,1:T(8,128)(2,1)} %copy.57), calls=%async_computation.1 | async-start | bytes 6291456 | tf_op jit(solution)/shard_map/all_to_all | solution.py:96
